TPU v7x, 128 devices: a whole 4x4x4 slice. The times are simulated.
128 devices in a mesh: req: 8 (over y, core), exp: 16 (over z, x).
Axes of the slice: x: 4, y: 4, z: 4, core: 2. Of those that a mesh axis runs over, the one named last changes fastest.
Arguments:
- hidden: bfloat16 [16384, 2560], P(('req', 'exp')), may hold values from -1.5 to 1.5
- queries: bfloat16 [16384, 1280], P(('req', 'exp')), may hold values from -100 to 100
- suffix_kv: bfloat16 [16384, 512], P(('req', 'exp')), may hold values from -24 to 24
- lengths: int32 [8, 4], P('req'), may hold values from 1 to 1024, 2048 in all within a row
- page_table: int32 [8, 4, 32], P('req'), may hold values from 0 to 55
- page_pool: bfloat16 [56, 128, 512], P('req'), may hold values from -24 to 24
- w_out: bfloat16 [1280, 2560], replicated, may hold values from -0.15625 to 0.15625
- w_router: bfloat16 [2560, 64], replicated, may hold values from -5 to 5
- routes: int32 [16384, 6], P(('req', 'exp')), may hold values from 0 to 63, all different within a row; in each aligned block of 128 rows (0 to 127, 128 to 255, ...) at most 15 rows name the same one
- w_gate: bfloat16 [128, 2560, 768], P(('req', 'exp')), may hold values from -0.125 to 0.125
- w_up: bfloat16 [128, 2560, 768], P(('req', 'exp')), may hold values from -0.125 to 0.125
- w_down: bfloat16 [128, 768, 2560], P(('req', 'exp')), may hold values from -0.4375 to 0.4375
Outputs:
- layer_out: bfloat16 [16384, 2560], P(('req', 'exp'))
Inputs may be any that keep to these rules, and one draw needn't show every extreme that they name: `lengths`: each row sums to 2048; its largest entry is exactly 1024. `page_table`: a page may appear in several prefixes and more than once in one. `routes`: the 6 experts of a token are distinct; among the rows of one device no expert is named more than 15 times, a bound that some block reaches.
All inputs are finite; a program needn't handle non-finite values.
Results may differ from a plain program's by a relative error of at most 0.022.
Values may be sent and summed in bfloat16 or wider, within the bound.
No kernel may reach another device: no remote copies, remote signals or barrier semaphores. Data moves between devices by JAX's collectives and lax.ppermute only.
A program may use at most 192 MiB of HBM per device.

v0:
```python
import math
import jax
import jax.numpy as jnp
from jax import lax
from jax.sharding import PartitionSpec as P

D = 2560
QUERY_HEADS = 10
KEY_VALUE_HEADS = 2
HEAD_SIZE = 128
TOP = 6
PAGE_TOKENS = 128
NEGATIVE_MASK = -1e30
EPS = 1e-06


def fold_scores(carry, query_matrix, key_rows, value_rows, weights):
    scores = jnp.einsum(
        "tgrd,kgd->tgrk", query_matrix, key_rows, preferred_element_type=jnp.float32
    ) * (1.0 / math.sqrt(HEAD_SIZE))
    running_maximum, grand_total, summed_output = carry
    live = weights[:, None, None, :] > 0
    fresh = jnp.maximum(running_maximum, jnp.max(jnp.where(live, scores, NEGATIVE_MASK), axis=-1))
    expo = jnp.where(live, jnp.exp(scores - fresh[..., None]), 0.0) * weights[:, None, None, :]
    decay = jnp.exp(running_maximum - fresh)
    grand_total = decay * grand_total + jnp.sum(expo, axis=-1)
    summed_output = decay[..., None] * summed_output + jnp.einsum(
        "tgrk,kgd->tgrd", expo.astype(jnp.bfloat16), value_rows, preferred_element_type=jnp.float32
    )
    return (fresh, grand_total, summed_output)


def empty_carry(token_count, request_groups):
    return (
        jnp.full((token_count, KEY_VALUE_HEADS, request_groups), NEGATIVE_MASK, jnp.float32),
        jnp.zeros((token_count, KEY_VALUE_HEADS, request_groups), jnp.float32),
        jnp.zeros((token_count, KEY_VALUE_HEADS, request_groups, HEAD_SIZE), jnp.float32),
    )


def on_device(
    hidden,
    queries,
    suffix_kv,
    lengths,
    page_table,
    page_pool,
    w_out,
    w_router,
    routes,
    w_gate,
    w_up,
    w_down,
):
    token_index = hidden.shape[0]
    row_width = KEY_VALUE_HEADS * HEAD_SIZE
    request_groups = QUERY_HEADS // KEY_VALUE_HEADS
    request_count = lax.axis_size("req")
    pool_per_shard = page_pool.shape[0]
    pool_all = pool_per_shard * request_count
    query_matrix = queries.reshape(token_index, KEY_VALUE_HEADS, request_groups, HEAD_SIZE)
    positions = lax.axis_index("exp") * token_index + jnp.arange(token_index, dtype=jnp.int32)
    lens = lengths[0]
    ends = jnp.cumsum(lens)
    starts = ends - lens
    req_of = jnp.sum((positions[:, None] >= ends[None, :]).astype(jnp.int32), axis=1)
    pick = req_of[:, None] == jnp.arange(lens.shape[0], dtype=jnp.int32)[None, :]
    first = jnp.sum(jnp.where(pick, starts[None, :], 0), axis=1)
    counts = jnp.sum(
        (page_table[0][:, :, None] == jnp.arange(pool_all, dtype=jnp.int32)[None, None, :]).astype(
            jnp.float32
        ),
        axis=1,
    )
    query_counts = jnp.dot(pick.astype(jnp.float32), counts, precision=lax.Precision.HIGHEST)
    query_total_set, every_count = (
        lax.all_gather(queries, "req", axis=0, tiled=True),
        lax.all_gather(query_counts.astype(jnp.bfloat16), "req", axis=0, tiled=True),
    )
    query_total_count = query_total_set.shape[0]
    local = lax.dynamic_slice_in_dim(
        every_count, lax.axis_index("req") * pool_per_shard, pool_per_shard, 1
    ).astype(jnp.float32)
    weights = jnp.repeat(local, PAGE_TOKENS, axis=1)
    flattened = page_pool.reshape(pool_per_shard * PAGE_TOKENS, 2 * row_width)
    key_rows = flattened[:, :row_width].reshape(
        pool_per_shard * PAGE_TOKENS, KEY_VALUE_HEADS, HEAD_SIZE
    )
    value_rows = flattened[:, row_width:].reshape(
        pool_per_shard * PAGE_TOKENS, KEY_VALUE_HEADS, HEAD_SIZE
    )
    running_maximum, grand_total, summed_output = fold_scores(
        empty_carry(query_total_count, request_groups),
        query_total_set.reshape(query_total_count, KEY_VALUE_HEADS, request_groups, HEAD_SIZE),
        key_rows,
        value_rows,
        weights,
    )
    peaks, totals, sums = (
        lax.all_to_all(
            running_maximum.reshape(request_count, token_index, KEY_VALUE_HEADS, request_groups),
            "req",
            split_axis=0,
            concat_axis=0,
            tiled=True,
        ),
        lax.all_to_all(
            grand_total.reshape(request_count, token_index, KEY_VALUE_HEADS, request_groups),
            "req",
            split_axis=0,
            concat_axis=0,
            tiled=True,
        ),
        lax.all_to_all(
            summed_output.reshape(
                request_count, token_index, KEY_VALUE_HEADS, request_groups, HEAD_SIZE
            ),
            "req",
            split_axis=0,
            concat_axis=0,
            tiled=True,
        ),
    )
    highest = jnp.max(peaks, axis=0)
    factor = jnp.exp(peaks - highest[None])
    carry = (highest, jnp.sum(factor * totals, axis=0), jnp.sum(factor[..., None] * sums, axis=0))
    segment = lax.all_gather(suffix_kv, "exp", axis=0, tiled=True)
    token_count = segment.shape[0]
    keypos = jnp.arange(token_count, dtype=jnp.int32)
    weights = (
        (keypos[None, :] <= positions[:, None]) & (keypos[None, :] >= first[:, None])
    ).astype(jnp.float32)
    key_rows = segment[:, :row_width].reshape(token_count, KEY_VALUE_HEADS, HEAD_SIZE)
    value_rows = segment[:, row_width:].reshape(token_count, KEY_VALUE_HEADS, HEAD_SIZE)
    running_maximum, grand_total, summed_output = fold_scores(
        carry, query_matrix, key_rows, value_rows, weights
    )
    attended = (
        (summed_output / grand_total[..., None])
        .reshape(token_index, QUERY_HEADS * HEAD_SIZE)
        .astype(jnp.bfloat16)
    )
    projected = jnp.dot(attended, w_out, preferred_element_type=jnp.float32)
    resid = lax.optimization_barrier((hidden.astype(jnp.float32) + projected).astype(jnp.bfloat16))
    resid_f = resid.astype(jnp.float32)
    normed = (resid_f * lax.rsqrt(jnp.mean(resid_f * resid_f, axis=1, keepdims=True) + EPS)).astype(
        jnp.bfloat16
    )
    n_experts = w_router.shape[1]
    logits = jnp.dot(normed, w_router, preferred_element_type=jnp.float32)
    expert_ids = jnp.arange(n_experts, dtype=jnp.int32)
    chosen = jnp.sum(
        jnp.where(routes[:, :, None] == expert_ids[None, None, :], logits[:, None, :], 0.0), axis=2
    )
    gates = jax.nn.softmax(chosen, axis=1)
    capacity = 16
    member = routes[:, :, None] == expert_ids[None, None, :]
    picks = jnp.any(member, axis=1).astype(jnp.float32)
    gate_of = jnp.sum(jnp.where(member, gates[:, :, None], 0.0), axis=1)
    earlier = (
        jnp.arange(token_index, dtype=jnp.int32)[:, None]
        > jnp.arange(token_index, dtype=jnp.int32)[None, :]
    ).astype(jnp.float32)
    rank = jnp.dot(earlier, picks, precision=lax.Precision.HIGHEST).astype(jnp.int32)
    place = jnp.arange(capacity, dtype=jnp.int32)
    select = (picks[None, :, :] > 0) & (rank[None, :, :] == place[:, None, None])
    select = jnp.transpose(select, (2, 0, 1))
    select2 = jnp.broadcast_to(select[:, None], (n_experts, 2, capacity, token_index)).reshape(
        2 * n_experts * capacity, token_index
    )
    outgoing = jnp.dot(
        select2.astype(jnp.bfloat16), normed, preferred_element_type=jnp.float32
    ).astype(jnp.bfloat16)
    outgoing = outgoing.reshape(2 * n_experts, capacity, D)
    rows = lax.all_to_all(outgoing, ("req", "exp"), split_axis=0, concat_axis=0, tiled=True)
    array_shape = rows.shape
    flat_rows = rows.reshape(-1, D)
    gate_part = jnp.dot(flat_rows, w_gate[0], preferred_element_type=jnp.float32)
    up_part = jnp.dot(flat_rows, w_up[0], preferred_element_type=jnp.float32)
    inner = (jax.nn.silu(gate_part) * up_part).astype(jnp.bfloat16)
    returned = lax.all_to_all(
        jnp.dot(inner, w_down[0], preferred_element_type=jnp.float32)
        .astype(jnp.bfloat16)
        .reshape(array_shape),
        ("req", "exp"),
        split_axis=0,
        concat_axis=0,
        tiled=True,
    ).reshape(2 * n_experts * capacity, D)
    weight = jnp.where(
        jnp.transpose(select, (2, 0, 1))[:, :, None, :], gate_of[:, :, None, None], 0.0
    )
    weight = jnp.broadcast_to(weight, (token_index, n_experts, 2, capacity)).reshape(
        token_index, 2 * n_experts * capacity
    )
    high = weight.astype(jnp.bfloat16)
    low = (weight - high.astype(jnp.float32)).astype(jnp.bfloat16)
    moe = jnp.dot(high, returned, preferred_element_type=jnp.float32) + jnp.dot(
        low, returned, preferred_element_type=jnp.float32
    )
    return (resid_f + moe).astype(jnp.bfloat16)


def solution(mesh):
    placed = (
        P(("req", "exp"), None),
        P(("req", "exp"), None),
        P(("req", "exp"), None),
        P("req", None),
        P("req", None, None),
        P("req", None, None),
        P(),
        P(),
        P(("req", "exp"), None),
        P(("req", "exp"), None, None),
        P(("req", "exp"), None, None),
        P(("req", "exp"), None, None),
    )
    return jax.shard_map(
        on_device, mesh=mesh, in_specs=placed, out_specs=P(("req", "exp"), None), check_vma=False
    )
```

profile of v0, /device:TPU:34, one launch (start us, length us, event | category | flops | bytes accessed | tf_op | source)
XLA Modules:
  0.0 531.8 jit_solution(14392213772407807917)
XLA Ops:
  7.4 0.0 copy-start
  7.4 0.0 all-gather.3.cloned.1.call-start
  7.4 1.9 copy.140
  9.3 0.0 all-gather.3.cloned.1.call-update
  9.3 0.8 reduce-window.4
  10.2 0.1 convert_reduce_fusion.1
  10.2 0.8 convert_reduce_fusion
  11.0 0.2 convolution_convert_fusion.3
  11.2 12.1 %all_gather.9 = bf16[1024,56]{0,1:T(8,128)(2,1)S(1)} all-gather(bf16[128,56]{0,1:T(8,128)(2,1)S(1)} %convolution_convert_fusion.3), channel_id=1, replica_groups=mesh['req'=8,'exp'=16] {'req'}, dimensions={0}, use_global_device_ids=true | all-gather | bytes 129024 | tf_op jit(solution)/shard_map/all_gather | solution.py:78
  23.4 0.2 bitcast_compare_fusion
  23.6 1.2 fusion.69
  24.8 0.2 copy.139
  25.1 16.3 %all-gather.3.cloned.1.call-done = bf16[1024,1280]{0,1:T(8,128)(2,1)} async-done(((bf16[128,1280]{0,1:T(8,128)(2,1)}), bf16[1024,1280]{0,1:T(8,128)(2,1)}) %all-gather.3.cloned.1.call-update) | async-done | bytes 2621456 | tf_op jit(solution)/shard_map/all_gather | solution.py:77
  41.4 16.3 %fusion = (f32[1024,2,5]{0,2,1:T(8,128)S(1)}, f32[2,896,1024,5]{2,1,3,0:T(8,128)}) fusion(pred[1024,896]{0,1:T(8,128)(4,1)S(1)} %bitcast_compare_fusion, bf16[896,2,128,1]{0,2,3,1:T(8,128)(2,1)S(1)} %bitcast.144, bf16[1024,2,5,128]{0,3,2,1:T(8,128)(2,1)} %bitcast.138), kind=kOutput, calls=%fused_computation.2 | convolution fusion | flops 2376325120 | bytes 40738816 | tf_op jit(solution)/shard_map/tgrd,kgd->tgrk/dot_general | solution.py:18
  57.7 0.4 broadcast_in_dim.146
  58.2 1.8 copy-done.1
  60.0 15.7 %fusion.4 = f32[1024,2,5]{0,2,1:T(8,128)S(1)} fusion(f32[2,896,1024,5]{2,1,3,0:T(8,128)} %get-tuple-element.20, f32[1024,896]{0,1:T(8,128)S(1)} %bitcast.133, f32[1024,2,5]{0,2,1:T(8,128)S(1)} %get-tuple-element.14, pred[1024,896]{0,1:T(8,128)(4,1)S(1)} %bitcast_compare_fusion), kind=kLoop, calls=%fused_computation.6 | loop fusion | flops 45864960 | bytes 41369600 | tf_op jit(solution)/shard_map/reduce_sum | solution.py:26
  75.7 0.6 copy.164
  76.3 4.0 all-to-all-start.2
  80.3 0.0 all-gather.5.cloned.1.call-start
  80.4 0.8 copy.146
  81.2 0.0 all-gather.5.cloned.1.call-update
  81.2 0.2 copy.155
  81.4 0.6 copy.144
  82.1 3.8 all-to-all-done.2
  85.8 3.3 all-to-all-start
  89.2 17.4 %bitcast_add_fusion = f32[1024,2,5,128]{3,0,2,1:T(8,128)S(1)} fusion(f32[1024,2,5]{0,2,1:T(8,128)S(1)} %get-tuple-element.13, bf16[896,2,128,1]{0,2,3,1:T(8,128)(2,1)S(1)} %bitcast.150, f32[2,896,1024,5]{2,1,3,0:T(8,128)} %get-tuple-element.20, f32[1024,896]{0,1:T(8,128)} %bitcast.134, f32[1024,2,5]{0,2,1:T(8,128)S(1)} %get-tuple-element.14, ...), kind=kOutput, calls=%fused_computation.21 | convolution fusion | flops 2395996160 | bytes 47071232 | tf_op jit(solution)/shard_map/tgrk,kgd->tgrd/dot_general | solution.py:27
  106.6 0.0 copy-start.9
  106.6 0.0 copy-start.7
  106.7 2.7 copy.158
  109.4 0.0 all-to-all-done
  109.4 5.0 all-to-all-start.1
  114.4 0.1 select_reduce_fusion.2
  114.4 0.0 copy-done.7
  114.5 0.1 convolution_convert_fusion.2
  114.6 0.1 fusion.47
  114.8 0.3 broadcast_compare_fusion
  115.1 0.0 copy-start.4
  115.1 15.4 %all-gather.5.cloned.1.call-done = bf16[2048,512]{0,1:T(8,128)(2,1)} async-done(((bf16[128,512]{0,1:T(8,128)(2,1)}), bf16[2048,512]{0,1:T(8,128)(2,1)}) %all-gather.5.cloned.1.call-update) | async-done | bytes 2097168 | tf_op jit(solution)/shard_map/all_gather | solution.py:127
  130.5 2.7 fusion.68
  133.2 5.8 %fusion.9 = (f32[128,2,5]{0,2,1:T(8,128)S(1)}, f32[2,2048,128,5]{2,1,3,0:T(8,128)}) fusion(pred[128,2048]{0,1:T(8,128)(4,1)S(1)} %get-tuple-element.17, bf16[2048,2,128,1]{0,2,3,1:T(8,128)(2,1)S(1)} %bitcast.141, bf16[128,2,5,128]{0,3,2,1:T(8,128)(2,1)S(1)} %bitcast.140), kind=kOutput, calls=%fused_computation.14 | convolution fusion | flops 678951680 | bytes 12129280 | tf_op jit(solution)/shard_map/tgrd,kgd->tgrk/dot_general | solution.py:18
  139.2 6.4 %fusion.13 = f32[128,2,5]{0,2,1:T(8,128)S(1)} fusion(f32[2,2048,128,5]{2,1,3,0:T(8,128)} %get-tuple-element.22, f32[128,2048]{0,1:T(8,128)S(1)} %get-tuple-element.18, f32[128,2,5]{0,2,1:T(8,128)S(1)} %copy.161, pred[128,2048]{0,1:T(8,128)(4,1)S(1)} %get-tuple-element.17), kind=kLoop, calls=%fused_computation.18 | loop fusion | flops 13105920 | bytes 11806720 | tf_op jit(solution)/shard_map/reduce_sum | solution.py:26
  145.7 29.6 %all-to-all-done.1 = f32[8,128,2,5,128]{4,1,3,2,0:T(8,128)} async-done(((f32[8,128,2,5,128]{4,1,3,2,0:T(8,128)}), f32[8,128,2,5,128]{4,1,3,2,0:T(8,128)}, u32[]{:S(2)}, u32[]{:S(2)}) %all-to-all-start.1) | async-done | bytes 5242912 | tf_op jit(solution)/shard_map/all_to_all | solution.py:114
  175.3 4.3 multiply_reduce_fusion
  179.6 2.2 copy.160
  181.8 7.9 %fusion.42 = bf16[128,2,5,128]{0,3,2,1:T(8,128)(2,1)S(1)} fusion(bf16[2048,2,128,1]{0,2,3,1:T(8,128)(2,1)} %bitcast.147, f32[2,2048,128,5]{2,1,3,0:T(8,128)} %get-tuple-element.22, f32[128,2048]{0,1:T(8,128)} %copy-done.4, f32[128,2,5]{0,2,1:T(8,128)S(1)} %copy.161, pred[128,2048]{0,1:T(8,128)(4,1)S(1)} %get-tuple-element.17, ...), kind=kOutput, calls=%fused_computation.49 | convolution fusion | flops 684851200 | bytes 13843456 | tf_op jit(solution)/shard_map/tgrk,kgd->tgrd/dot_general | solution.py:27
  189.7 1.0 fusion.25
  190.7 0.2 fusion.29
  191.0 0.1 broadcast_in_dim.166
  191.0 3.2 convolution_convert_fusion.1
  194.3 0.0 copy-start.8
  194.3 126.3 %all_to_all.25 = bf16[128,16,2560]{2,1,0:T(8,128)(2,1)S(1)} all-to-all(bf16[128,16,2560]{2,1,0:T(8,128)(2,1)S(1)} %bitcast.130), channel_id=1, replica_groups=mesh['req'=8,'exp'=16] {'req','exp'}, dimensions={0} | all-to-all | bytes 20971520 | tf_op jit(solution)/shard_map/all_to_all | solution.py:175
  320.5 3.8 copy-done.2
  324.4 10.2 %fusion.21 = f32[2048,768]{1,0:T(8,128)} fusion(bf16[2048,2560]{1,0:T(8,128)(2,1)S(1)} %bitcast.136, bf16[1,2560,768]{2,1,0:T(8,128)(2,1)S(1)} %copy-done.8), kind=kOutput, calls=%fused_computation.27 | convolution fusion | flops 8053063680 | bytes 20709376 | tf_op jit(solution)/shard_map/dot_general | solution.py:178
  334.5 28.9 %convolution_convert_fusion = bf16[2048,2560]{1,0:T(8,128)(2,1)} fusion(f32[2048,768]{1,0:T(8,128)} %fusion.21, bf16[2048,2560]{1,0:T(8,128)(2,1)} %bitcast.137, bf16[1,768,2560]{2,1,0:T(8,128)(2,1)} %param.23, bf16[1,2560,768]{2,1,0:T(8,128)(2,1)} %param.22), kind=kOutput, calls=%fused_computation.10 | convolution fusion | flops 16120807424 | bytes 35127296 | tf_op jit(solution)/shard_map/dot_general | solution.py:182
  363.5 6.7 %all-to-all-start.4 = ((bf16[128,16,2560]{2,1,0:T(8,128)(2,1)}), bf16[128,16,2560]{2,1,0:T(8,128)(2,1)}, u32[]{:S(2)}, u32[]{:S(2)}) async-start(bf16[128,16,2560]{2,1,0:T(8,128)(2,1)} %bitcast.135), calls=%async_computation.4 | async-start | bytes 20971520 | tf_op jit(solution)/shard_map/all_to_all | solution.py:181
  370.1 0.4 fusion.49
  370.7 0.1 select_convert_fusion
  370.8 0.1 fusion.45
  371.0 141.3 %all-to-all-done.4 = bf16[128,16,2560]{2,1,0:T(8,128)(2,1)} async-done(((bf16[128,16,2560]{2,1,0:T(8,128)(2,1)}), bf16[128,16,2560]{2,1,0:T(8,128)(2,1)}, u32[]{:S(2)}, u32[]{:S(2)}) %all-to-all-start.4) | async-done | bytes 10485792 | tf_op jit(solution)/shard_map/all_to_all | solution.py:181
  512.3 0.1 broadcast_in_dim.165
  512.3 5.5 %fusion.70 = f32[128,2560]{1,0:T(8,128)S(1)} fusion(bf16[128,2048]{0,1:T(8,128)(2,1)S(1)} %bitcast.143, bf16[2048,2560]{1,0:T(8,128)(2,1)} %bitcast.34), kind=kOutput, calls=%fused_computation.101 | convolution fusion | flops 1342177280 | bytes 12320768 | tf_op jit(solution)/shard_map/dot_general | solution.py:198
  517.9 0.1 broadcast_in_dim.167
  518.0 6.4 %fusion.24 = bf16[128,2560]{1,0:T(8,128)(2,1)} fusion(f32[128,2560]{1,0:T(8,128)S(1)} %fusion.70, bf16[128,2048]{0,1:T(8,128)(2,1)S(1)} %bitcast.142, bf16[2048,2560]{1,0:T(8,128)(2,1)} %bitcast.34, bf16[128,2560]{1,0:T(8,128)(2,1)S(1)} %fusion.25), kind=kOutput, calls=%fused_computation.32 | convolution fusion | flops 1343488000 | bytes 13631488 | tf_op jit(solution)/shard_map/dot_general | solution.py:198
  (41 shorter events, 0.4 us)
Async XLA Ops:
  7.4 362.8 %copy-start = (bf16[2560,64]{0,1:T(8,128)(2,1)S(1)}, bf16[2560,64]{0,1:T(8,128)(2,1)}, u32[]{:S(2)}) copy-start(bf16[2560,64]{0,1:T(8,128)(2,1)} %param.19) | copy-start | bytes 983044
  7.4 34.0 %all-gather.3.cloned.1.call-start = ((), (), s32[]{:S(2)}) async-start(), calls=%async_computation.5 | async-start | bytes 2949120 | tf_op jit(solution)/shard_map/all_gather | solution.py:77
  58.2 1.8 copy-start.1
  60.0 20.4 %copy-start.6 = (bf16[128,512]{1,0:T(8,128)(2,1)S(1)}, bf16[128,512]{1,0:T(8,128)(2,1)}, u32[]{:S(2)}) copy-start(bf16[128,512]{1,0:T(8,128)(2,1)} %param.14) | copy-start | bytes 393220
  76.3 9.5 %all-to-all-start.2 = ((f32[8,128,2,5]{1,2,3,0:T(2,128)}), f32[8,128,2,5]{1,2,3,0:T(2,128)S(1)}, u32[]{:S(2)}, u32[]{:S(2)}) async-start(f32[8,128,2,5]{1,2,3,0:T(2,128)} %copy.164), calls=%async_computation.2 | async-start | bytes 81920 | tf_op jit(solution)/shard_map/all_to_all | solution.py:107
  80.3 50.2 %all-gather.5.cloned.1.call-start = ((), (), s32[]{:S(2)}) async-start(), calls=%async_computation.6 | async-start | bytes 2228224 | tf_op jit(solution)/shard_map/all_gather | solution.py:127
  85.8 23.6 %all-to-all-start = ((f32[8,128,2,5]{1,2,3,0:T(2,128)}), f32[8,128,2,5]{1,2,3,0:T(2,128)S(1)}, u32[]{:S(2)}, u32[]{:S(2)}) async-start(f32[8,128,2,5]{1,2,3,0:T(2,128)} %copy.144), calls=%async_computation | async-start | bytes 81920 | tf_op jit(solution)/shard_map/all_to_all | solution.py:100
  106.6 7.7 %copy-start.9 = (s32[1,4]{1,0:T(1,128)S(1)}, s32[1,4]{1,0:T(1,128)}, u32[]{:S(2)}) copy-start(s32[1,4]{1,0:T(1,128)} %param.15) | copy-start | bytes 52
  106.6 7.8 %copy-start.7 = (s32[128,6]{0,1:T(8,128)S(1)}, s32[128,6]{0,1:T(8,128)}, u32[]{:S(2)}) copy-start(s32[128,6]{0,1:T(8,128)} %param.20) | copy-start | bytes 9220
  109.4 23.9 %copy-start.3 = (bf16[128,1280]{0,1:T(8,128)(2,1)S(1)}, bf16[128,1280]{0,1:T(8,128)(2,1)}, u32[]{:S(2)}) copy-start(bf16[128,1280]{0,1:T(8,128)(2,1)} %copy.140) | copy-start | bytes 983044
  109.4 65.9 %all-to-all-start.1 = ((f32[8,128,2,5,128]{4,1,3,2,0:T(8,128)}), f32[8,128,2,5,128]{4,1,3,2,0:T(8,128)}, u32[]{:S(2)}, u32[]{:S(2)}) async-start(f32[8,128,2,5,128]{4,1,3,2,0:T(8,128)} %copy.158), calls=%async_computation.1 | async-start | bytes 10485760 | tf_op jit(solution)/shard_map/all_to_all | solution.py:114
  115.1 24.1 %copy-start.4 = (f32[128,2048]{0,1:T(8,128)}, f32[128,2048]{0,1:T(8,128)S(1)}, u32[]{:S(2)}) copy-start(f32[128,2048]{0,1:T(8,128)S(1)} %get-tuple-element.18) | copy-start | bytes 3145732
  175.3 14.4 %slice-start = ((s8[6553600]{0:T(1024)(128)(4,1)}), s8[2359296]{0:T(1024)(128)(4,1)S(1)}, s32[]{:S(2)}) async-start(s8[6553600]{0:T(1024)(128)(4,1)} %bitcast.131), calls=%async_computation.7 | async-start | bytes 4718592
  181.8 7.9 %slice-start.1 = ((s8[6553600]{0:T(1024)(128)(4,1)}), s8[4194304]{0:T(1024)(128)(4,1)S(1)}, s32[]{:S(2)}) async-start(s8[6553600]{0:T(1024)(128)(4,1)} %bitcast.131), calls=%async_computation.8 | async-start | bytes 8388608
  181.8 7.9 %copy-start.5 = (bf16[128,2560]{1,0:T(8,128)(2,1)S(1)}, bf16[128,2560]{1,0:T(8,128)(2,1)}, u32[]{:S(2)}) copy-start(bf16[128,2560]{1,0:T(8,128)(2,1)} %param.12) | copy-start | bytes 1966084
  194.3 130.1 %copy-start.8 = (bf16[1,2560,768]{2,1,0:T(8,128)(2,1)S(1)}, bf16[1,2560,768]{2,1,0:T(8,128)(2,1)}, u32[]{:S(2)}) copy-start(bf16[1,2560,768]{2,1,0:T(8,128)(2,1)} %param.21) | copy-start | bytes 11796484
  320.5 3.8 copy-start.2
  363.5 148.8 %all-to-all-start.4 = ((bf16[128,16,2560]{2,1,0:T(8,128)(2,1)}), bf16[128,16,2560]{2,1,0:T(8,128)(2,1)}, u32[]{:S(2)}, u32[]{:S(2)}) async-start(bf16[128,16,2560]{2,1,0:T(8,128)(2,1)} %bitcast.135), calls=%async_computation.4 | async-start | bytes 20971520 | tf_op jit(solution)/shard_map/all_to_all | solution.py:181
Sparse Core Ops, SparseCore 0:
  9.9 31.4 all-gather.2
Sparse Core Ops, SparseCore 1:
  82.9 47.5 all-gather.4
where the time goes:
time: 533 us; the launch traced here: 532 us
  waiting for transfers between devices  206 us (39%)
  blocking collectives  138 us (26%)
  matrix products  104 us (20%)
  other arithmetic  29.7 us (6%)
  local copies, waits for them, and re-layouts  19.7 us (4%)
  starting transfers between devices  19 us (4%)
  between operations  15.2 us (3%)
    all_to_all x1, waiting for transfers between devices, on_device(): lax.all_to_all(jnp.dot(inner, w_down[0], preferred_element_type=jnp.float...  141 us
    all_to_all x1, blocking collectives, on_device(): lax.all_to_all(outgoing, ('req', 'exp'), split_axis=0, concat_axis=0, til...  126 us
    all_to_all x1, waiting for transfers between devices, on_device(): lax.all_to_all(summed_output.reshape(request_count, token_index, KEY_VALU...  29.6 us
    dot_general x1, matrix products, on_device(): jnp.dot(inner, w_down[0], preferred_element_type=jnp.float32)  28.9 us
    dot_general x2, matrix products, fold_scores(): jnp.einsum('tgrk,kgd->tgrd', expo.astype(jnp.bfloat16), value_rows, prefe...  25.3 us
    dot_general x2, matrix products, fold_scores(): jnp.einsum('tgrd,kgd->tgrk', query_matrix, key_rows, preferred_element_ty...  22.1 us
    reduce_sum x2, other arithmetic, fold_scores(): grand_total = decay * grand_total + jnp.sum(expo, axis=-1)  22.1 us
    all_gather x1, waiting for transfers between devices, on_device(): lax.all_gather(queries, 'req', axis=0, tiled=True)  16.3 us
  transfers between devices with their start and end apart: 6, of which 5 were waited for; matrix products, arithmetic and copies ran while one was open for 8% of the time, Pallas kernels for 0%

commit v1 on v0

--- a/solution.py
+++ b/solution.py
@@ -1,3 +1,4 @@
+import functools
 import math
 import jax
 import jax.numpy as jnp
@@ -12,6 +13,35 @@
 PAGE_TOKENS = 128
 NEGATIVE_MASK = -1e30
 EPS = 1e-06
+
+
+def guide_the_field(patch, dim_no):
+    vec_out = jax.lax.axis_size("exp")
+    then, w_next, seen_now = (vec_out, jax.lax.axis_index("exp"), patch.shape[dim_no])
+    table = tuple(((dd, (dd + 1) % then) for dd in range(then)))
+    vals = tuple(((dd, (dd - 1) % then) for dd in range(then)))
+    f_now = jnp.zeros(
+        (*patch.shape[:dim_no], then * seen_now, *patch.shape[dim_no + 1 :]), patch.dtype
+    )
+    f_now = lax.dynamic_update_slice_in_dim(f_now, patch, w_next * seen_now, axis=dim_no)
+    mid_arr = x_next = patch
+    mixed_arr = then // 2
+    p = 1
+    while p < mixed_arr + 1:
+        mid_arr = jax.lax.ppermute(mid_arr, axis_name="exp", perm=table)
+        f_now = lax.dynamic_update_slice_in_dim(
+            f_now, mid_arr, (w_next - p) % then * seen_now, axis=dim_no
+        )
+        if p < then - mixed_arr:
+            x_next = jax.lax.ppermute(x_next, axis_name="exp", perm=vals)
+            f_now = lax.dynamic_update_slice_in_dim(
+                f_now, x_next, (w_next + p) % then * seen_now, axis=dim_no
+            )
+        p += 1
+    return f_now
+
+
+turn_the_zone = functools.partial(guide_the_field, dim_no=0)
 
 
 def fold_scores(carry, query_matrix, key_rows, value_rows, weights):
@@ -124,7 +154,7 @@
     highest = jnp.max(peaks, axis=0)
     factor = jnp.exp(peaks - highest[None])
     carry = (highest, jnp.sum(factor * totals, axis=0), jnp.sum(factor[..., None] * sums, axis=0))
-    segment = lax.all_gather(suffix_kv, "exp", axis=0, tiled=True)
+    segment = turn_the_zone(suffix_kv)
     token_count = segment.shape[0]
     keypos = jnp.arange(token_count, dtype=jnp.int32)
     weights = (

time: 533 us -> 560 us (1.051); the launches traced: 532 us -> 551 us
  starting transfers between devices: 19 us -> 55.8 us
  waiting for transfers between devices: 206 us -> 178 us
  blocking collectives: 138 us -> 147 us
    all_to_all x1, waiting for transfers between devices: 29.6 us -> 0.01 us  [on_device(): lax.all_to_all(summed_output.reshape(request_count, token_index, KEY_VALU...]
    ppermute x0 -> x15, waiting for transfers between devices: none -> 24.8 us  [the longest x8 24.8 us: guide_the_field(): mid_arr = jax.lax.ppermute(mid_arr, axis_name='exp', perm=table)]
    ppermute x0 -> x15, starting transfers between devices: none -> 23.2 us  [the longest x7 18.1 us: guide_the_field(): x_next = jax.lax.ppermute(x_next, axis_name='exp', perm=vals)]
    all_gather x1 -> x0, waiting for transfers between devices: 15.4 us -> none  [on_device(): segment = lax.all_gather(suffix_kv, 'exp', axis=0, tiled=True)]
    all_to_all x1, starting transfers between devices: 4.95 us -> 17 us  [on_device(): lax.all_to_all(summed_output.reshape(request_count, token_index, KEY_VALU...]
    all_to_all x1, blocking collectives: 126 us -> 134 us  [on_device(): lax.all_to_all(outgoing, ('req', 'exp'), split_axis=0, concat_axis=0, til...]
  transfers between devices with their start and end apart: 6 -> 20, of which waited for: 5 -> 9; matrix products, arithmetic and copies ran while one was open for 8% -> 14% of each run, Pallas kernels for 0% -> 0%
where the time goes in v1:
time: 560 us; the launch traced here: 551 us
  waiting for transfers between devices  178 us (32%)
  blocking collectives  147 us (26%)
  matrix products  104 us (19%)
  starting transfers between devices  55.8 us (10%)
  other arithmetic  30.9 us (6%)
  local copies, waits for them, and re-layouts  21.7 us (4%)
  between operations  14.6 us (3%)
    all_to_all x1, waiting for transfers between devices, on_device(): lax.all_to_all(jnp.dot(inner, w_down[0], preferred_element_type=jnp.float...  141 us
    all_to_all x1, blocking collectives, on_device(): lax.all_to_all(outgoing, ('req', 'exp'), split_axis=0, concat_axis=0, til...  134 us
    dot_general x1, matrix products, on_device(): jnp.dot(inner, w_down[0], preferred_element_type=jnp.float32)  28.9 us
    dot_general x2, matrix products, fold_scores(): jnp.einsum('tgrk,kgd->tgrd', expo.astype(jnp.bfloat16), value_rows, prefe...  25.5 us
    ppermute x8, waiting for transfers between devices, guide_the_field(): mid_arr = jax.lax.ppermute(mid_arr, axis_name='exp', perm=table)  24.8 us
    dot_general x2, matrix products, fold_scores(): jnp.einsum('tgrd,kgd->tgrk', query_matrix, key_rows, preferred_element_ty...  22.1 us
    reduce_sum x2, other arithmetic, fold_scores(): grand_total = decay * grand_total + jnp.sum(expo, axis=-1)  22.1 us
    ppermute x7, starting transfers between devices, guide_the_field(): x_next = jax.lax.ppermute(x_next, axis_name='exp', perm=vals)  18.1 us
  transfers between devices with their start and end apart: 20, of which 9 were waited for; matrix products, arithmetic and copies ran while one was open for 14% of the time, Pallas kernels for 0%

profile of v1, /device:TPU:34, one launch (start us, length us, event | category | flops | bytes accessed | tf_op | source)
XLA Modules:
  0.0 550.8 jit_solution(1584624167168252355)
XLA Ops:
  6.5 1.9 copy.165
  8.5 1.0 copy.171
  9.5 1.6 collective-permute-start
  11.1 0.5 collective-permute-start.1
  11.6 0.8 reduce-window.4
  12.5 0.8 convert_reduce_fusion
  13.3 0.2 convolution_convert_fusion.3
  13.5 12.1 %all_gather.6 = bf16[1024,56]{0,1:T(8,128)(2,1)S(1)} all-gather(bf16[128,56]{0,1:T(8,128)(2,1)S(1)} %convolution_convert_fusion.3), channel_id=1, replica_groups=mesh['req'=8,'exp'=16] {'req'}, dimensions={0}, use_global_device_ids=true | all-gather | bytes 129024 | tf_op jit(solution)/shard_map/all_gather | solution.py:108
  25.7 0.2 bitcast_compare_fusion
  25.9 1.2 fusion.69
  27.1 0.2 copy.164
  27.4 1.0 copy.182
  28.5 0.6 fusion.66
  29.2 0.3 broadcast_compare_fusion
  29.6 11.4 %all-gather.2.cloned.1.call-done = bf16[1024,1280]{0,1:T(8,128)(2,1)} async-done(((bf16[128,1280]{0,1:T(8,128)(2,1)}), bf16[1024,1280]{0,1:T(8,128)(2,1)}) %all-gather.2.cloned.1.call-update) | async-done | bytes 2621456 | tf_op jit(solution)/shard_map/all_gather | solution.py:107
  41.0 16.3 %fusion = (f32[1024,2,5]{0,2,1:T(8,128)S(1)}, f32[2,896,1024,5]{2,1,3,0:T(8,128)}) fusion(pred[1024,896]{0,1:T(8,128)(4,1)S(1)} %bitcast_compare_fusion, bf16[896,2,128,1]{0,2,3,1:T(8,128)(2,1)S(1)} %bitcast.144, bf16[1024,2,5,128]{0,3,2,1:T(8,128)(2,1)} %bitcast.138), kind=kOutput, calls=%fused_computation.2 | convolution fusion | flops 2376325120 | bytes 40738816 | tf_op jit(solution)/shard_map/tgrd,kgd->tgrk/dot_general | solution.py:48
  57.3 0.6 exponential_multiply_fusion
  58.0 0.6 copy.169
  58.6 4.0 all-to-all-start
  62.6 0.4 broadcast_in_dim.149
  63.1 1.8 copy-done.1
  64.9 15.7 %fusion.4 = f32[1024,2,5]{0,2,1:T(8,128)S(1)} fusion(f32[2,896,1024,5]{2,1,3,0:T(8,128)} %get-tuple-element.20, f32[1024,896]{0,1:T(8,128)S(1)} %bitcast.133, f32[1024,2,5]{0,2,1:T(8,128)S(1)} %get-tuple-element.14, pred[1024,896]{0,1:T(8,128)(4,1)S(1)} %bitcast_compare_fusion), kind=kLoop, calls=%fused_computation.6 | loop fusion | flops 45864960 | bytes 41369600 | tf_op jit(solution)/shard_map/reduce_sum | solution.py:56
  80.6 0.6 copy.191
  81.2 4.8 all-to-all-start.2
  86.1 17.6 %bitcast_add_fusion = f32[1024,2,5,128]{3,0,2,1:T(8,128)S(1)} fusion(f32[1024,2,5]{0,2,1:T(8,128)} %get-tuple-element.13, bf16[896,2,128,1]{0,2,3,1:T(8,128)(2,1)S(1)} %bitcast.150, f32[2,896,1024,5]{2,1,3,0:T(8,128)} %get-tuple-element.20, f32[1024,896]{0,1:T(8,128)} %bitcast.134, f32[1024,2,5]{0,2,1:T(8,128)S(1)} %get-tuple-element.14, ...), kind=kOutput, calls=%fused_computation.21 | convolution fusion | flops 2395996160 | bytes 47071232 | tf_op jit(solution)/shard_map/tgrk,kgd->tgrd/dot_general | solution.py:57
  103.7 2.7 copy.185
  106.4 17.0 %all-to-all-start.1 = ((f32[8,128,2,5,128]{4,1,3,2,0:T(8,128)}), f32[8,128,2,5,128]{4,1,3,2,0:T(8,128)}, u32[]{:S(2)}, u32[]{:S(2)}) async-start(f32[8,128,2,5,128]{4,1,3,2,0:T(8,128)} %copy.185), calls=%async_computation.1 | async-start | bytes 10485760 | tf_op jit(solution)/shard_map/all_to_all | solution.py:144
  123.9 0.2 broadcast_in_dim.157
  124.2 1.5 collective-permute-start.2
  125.7 0.6 collective-permute-start.3
  126.3 0.9 constant_dynamic-update-slice_fusion.14
  127.2 0.9 constant_dynamic-update-slice_fusion.13
  128.2 2.2 collective-permute-done.2
  130.3 1.5 collective-permute-start.4
  131.8 1.3 collective-permute-start.5
  133.2 3.4 collective-permute-done.4
  136.6 0.5 collective-permute-start.6
  137.0 3.4 collective-permute-start.7
  140.5 2.8 collective-permute-done.6
  143.4 4.1 collective-permute-start.9
  147.6 2.8 collective-permute-done.8
  150.4 4.1 collective-permute-start.11
  154.7 2.8 collective-permute-done.10
  157.5 4.1 collective-permute-start.13
  161.7 3.4 collective-permute-done.12
  165.3 7.3 %collective-permute-done.14 = bf16[128,512]{0,1:T(8,128)(2,1)S(1)} collective-permute-done((bf16[128,512]{0,1:T(8,128)(2,1)S(1)}, bf16[128,512]{0,1:T(8,128)(2,1)S(1)}, u32[]{:S(2)}, u32[]{:S(2)}) %collective-permute-start.14) | collective-permute-done | bytes 131104 | tf_op jit(solution)/shard_map/ppermute | solution.py:31
  172.6 1.1 fusion.68
  173.7 5.8 %fusion.9 = (f32[128,2,5]{0,2,1:T(8,128)S(1)}, f32[2,2048,128,5]{2,1,3,0:T(8,128)}) fusion(pred[128,2048]{0,1:T(8,128)(4,1)S(1)} %get-tuple-element.17, bf16[2048,2,128,1]{0,2,3,1:T(8,128)(2,1)S(1)} %bitcast.141, bf16[128,2,5,128]{0,3,2,1:T(8,128)(2,1)S(1)} %bitcast.140), kind=kOutput, calls=%fused_computation.14 | convolution fusion | flops 678951680 | bytes 12129280 | tf_op jit(solution)/shard_map/tgrd,kgd->tgrk/dot_general | solution.py:48
  179.7 6.4 %fusion.13 = f32[128,2,5]{0,2,1:T(8,128)S(1)} fusion(f32[2,2048,128,5]{2,1,3,0:T(8,128)} %get-tuple-element.22, f32[128,2048]{0,1:T(8,128)S(1)} %get-tuple-element.18, f32[128,2,5]{0,2,1:T(8,128)S(1)} %copy.188, pred[128,2048]{0,1:T(8,128)(4,1)S(1)} %get-tuple-element.17), kind=kLoop, calls=%fused_computation.18 | loop fusion | flops 13105920 | bytes 11806720 | tf_op jit(solution)/shard_map/reduce_sum | solution.py:56
  186.2 4.3 multiply_reduce_fusion
  190.5 2.2 copy.187
  192.7 7.9 %fusion.42 = bf16[128,2,5,128]{0,3,2,1:T(8,128)(2,1)S(1)} fusion(bf16[2048,2,128,1]{0,2,3,1:T(8,128)(2,1)} %bitcast.147, f32[2,2048,128,5]{2,1,3,0:T(8,128)} %get-tuple-element.22, f32[128,2048]{0,1:T(8,128)} %copy-done.4, f32[128,2,5]{0,2,1:T(8,128)S(1)} %copy.188, pred[128,2048]{0,1:T(8,128)(4,1)S(1)} %get-tuple-element.17, ...), kind=kOutput, calls=%fused_computation.49 | convolution fusion | flops 684851200 | bytes 13843456 | tf_op jit(solution)/shard_map/tgrk,kgd->tgrd/dot_general | solution.py:57
  200.6 1.1 fusion.25
  201.6 0.2 fusion.29
  201.9 3.2 convolution_convert_fusion.1
  205.2 134.4 %all_to_all.25 = bf16[128,16,2560]{2,1,0:T(8,128)(2,1)S(1)} all-to-all(bf16[128,16,2560]{2,1,0:T(8,128)(2,1)S(1)} %bitcast.130), channel_id=1, replica_groups=mesh['req'=8,'exp'=16] {'req','exp'}, dimensions={0} | all-to-all | bytes 20971520 | tf_op jit(solution)/shard_map/all_to_all | solution.py:205
  339.6 3.8 copy-done.2
  343.4 10.2 %fusion.21 = f32[2048,768]{1,0:T(8,128)} fusion(bf16[2048,2560]{1,0:T(8,128)(2,1)S(1)} %bitcast.136, bf16[1,2560,768]{2,1,0:T(8,128)(2,1)S(1)} %copy-done.10), kind=kOutput, calls=%fused_computation.27 | convolution fusion | flops 8053063680 | bytes 20709376 | tf_op jit(solution)/shard_map/dot_general | solution.py:208
  353.6 28.9 %convolution_convert_fusion = bf16[2048,2560]{1,0:T(8,128)(2,1)} fusion(f32[2048,768]{1,0:T(8,128)} %fusion.21, bf16[2048,2560]{1,0:T(8,128)(2,1)} %bitcast.137, bf16[1,768,2560]{2,1,0:T(8,128)(2,1)} %param.23, bf16[1,2560,768]{2,1,0:T(8,128)(2,1)} %param.22), kind=kOutput, calls=%fused_computation.10 | convolution fusion | flops 16120807424 | bytes 35127296 | tf_op jit(solution)/shard_map/dot_general | solution.py:212
  382.5 6.8 %all-to-all-start.4 = ((bf16[128,16,2560]{2,1,0:T(8,128)(2,1)}), bf16[128,16,2560]{2,1,0:T(8,128)(2,1)}, u32[]{:S(2)}, u32[]{:S(2)}) async-start(bf16[128,16,2560]{2,1,0:T(8,128)(2,1)} %bitcast.135), calls=%async_computation.4 | async-start | bytes 20971520 | tf_op jit(solution)/shard_map/all_to_all | solution.py:211
  389.3 0.4 fusion.49
  390.2 141.3 %all-to-all-done.4 = bf16[128,16,2560]{2,1,0:T(8,128)(2,1)} async-done(((bf16[128,16,2560]{2,1,0:T(8,128)(2,1)}), bf16[128,16,2560]{2,1,0:T(8,128)(2,1)}, u32[]{:S(2)}, u32[]{:S(2)}) %all-to-all-start.4) | async-done | bytes 10485792 | tf_op jit(solution)/shard_map/all_to_all | solution.py:211
  531.5 5.6 %fusion.70 = f32[128,2560]{1,0:T(8,128)S(1)} fusion(bf16[128,2048]{0,1:T(8,128)(2,1)S(1)} %bitcast.143, bf16[2048,2560]{1,0:T(8,128)(2,1)} %bitcast.34), kind=kOutput, calls=%fused_computation.117 | convolution fusion | flops 1342177280 | bytes 12320768 | tf_op jit(solution)/shard_map/dot_general | solution.py:228
  537.2 6.4 %fusion.24 = bf16[128,2560]{1,0:T(8,128)(2,1)} fusion(f32[128,2560]{1,0:T(8,128)S(1)} %fusion.70, bf16[128,2048]{0,1:T(8,128)(2,1)S(1)} %bitcast.142, bf16[2048,2560]{1,0:T(8,128)(2,1)} %bitcast.34, bf16[128,2560]{1,0:T(8,128)(2,1)S(1)} %fusion.25), kind=kOutput, calls=%fused_computation.32 | convolution fusion | flops 1343488000 | bytes 13631488 | tf_op jit(solution)/shard_map/dot_general | solution.py:228
  (89 shorter events, 1.9 us)
Async XLA Ops:
  6.5 382.8 %copy-start = (bf16[2560,64]{0,1:T(8,128)(2,1)S(1)}, bf16[2560,64]{0,1:T(8,128)(2,1)}, u32[]{:S(2)}) copy-start(bf16[2560,64]{0,1:T(8,128)(2,1)} %param.19) | copy-start | bytes 983044
  6.5 21.8 %copy-start.11 = (s32[1,4]{1,0:T(1,128)S(1)}, s32[1,4]{1,0:T(1,128)}, u32[]{:S(2)}) copy-start(s32[1,4]{1,0:T(1,128)} %param.15) | copy-start | bytes 52
  6.5 21.9 %copy-start.8 = (s32[128,6]{0,1:T(8,128)S(1)}, s32[128,6]{0,1:T(8,128)}, u32[]{:S(2)}) copy-start(s32[128,6]{0,1:T(8,128)} %param.20) | copy-start | bytes 9220
  6.5 34.5 %all-gather.2.cloned.1.call-start = ((), (), s32[]{:S(2)}) async-start(), calls=%async_computation.5 | async-start | bytes 2949120 | tf_op jit(solution)/shard_map/all_gather | solution.py:107
  9.5 114.6 %collective-permute-start = (bf16[128,512]{0,1:T(8,128)(2,1)S(1)}, bf16[128,512]{0,1:T(8,128)(2,1)}, u32[]{:S(2)}, u32[]{:S(2)}) collective-permute-start(bf16[128,512]{0,1:T(8,128)(2,1)S(1)} %copy.171), channel_id=1, source_target_pairs={{0,1},{1,2},{2,3},{3,4},{4,5},{5,6},{6,7},{7,8},{8,9},{9,10},{10,1... | collective-permute-start | bytes 393224 | tf_op jit(solution)/shard_map/ppermute | solution.py:31
  11.1 114.6 %collective-permute-start.1 = (bf16[128,512]{0,1:T(8,128)(2,1)S(1)}, bf16[128,512]{0,1:T(8,128)(2,1)}, u32[]{:S(2)}, u32[]{:S(2)}) collective-permute-start(bf16[128,512]{0,1:T(8,128)(2,1)S(1)} %copy.171), channel_id=1, source_target_pairs={{0,15},{1,0},{2,1},{3,2},{4,3},{5,4},{6,5},{7,6},{8,7},{9,8},{10,9... | collective-permute-start | bytes 393224 | tf_op jit(solution)/shard_map/ppermute | solution.py:36
  29.6 150.1 %copy-start.4 = (f32[128,2048]{0,1:T(8,128)}, f32[128,2048]{0,1:T(8,128)S(1)}, u32[]{:S(2)}) copy-start(f32[128,2048]{0,1:T(8,128)S(1)} %get-tuple-element.18) | copy-start | bytes 3145732
  58.6 22.6 %all-to-all-start = ((f32[8,128,2,5]{1,2,3,0:T(2,128)}), f32[8,128,2,5]{1,2,3,0:T(2,128)S(1)}, u32[]{:S(2)}, u32[]{:S(2)}) async-start(f32[8,128,2,5]{1,2,3,0:T(2,128)} %copy.169), calls=%async_computation | async-start | bytes 81920 | tf_op jit(solution)/shard_map/all_to_all | solution.py:130
  63.1 1.8 copy-start.1
  64.9 21.2 %copy-start.6 = (bf16[896,256]{0,1:T(8,128)(2,1)S(1)}, bf16[896,256]{0,1:T(8,128)(2,1)}, u32[]{:S(2)}) copy-start(bf16[896,256]{0,1:T(8,128)(2,1)} %copy.182) | copy-start | bytes 1376260
  81.2 25.2 %all-to-all-start.2 = ((f32[8,128,2,5]{1,2,3,0:T(2,128)}), f32[8,128,2,5]{1,2,3,0:T(2,128)S(1)}, u32[]{:S(2)}, u32[]{:S(2)}) async-start(f32[8,128,2,5]{1,2,3,0:T(2,128)} %copy.191), calls=%async_computation.2 | async-start | bytes 81920 | tf_op jit(solution)/shard_map/all_to_all | solution.py:137
  106.4 79.7 %all-to-all-start.1 = ((f32[8,128,2,5,128]{4,1,3,2,0:T(8,128)}), f32[8,128,2,5,128]{4,1,3,2,0:T(8,128)}, u32[]{:S(2)}, u32[]{:S(2)}) async-start(f32[8,128,2,5,128]{4,1,3,2,0:T(8,128)} %copy.185), calls=%async_computation.1 | async-start | bytes 10485760 | tf_op jit(solution)/shard_map/all_to_all | solution.py:144
  123.9 49.9 %copy-start.3 = (bf16[128,1280]{0,1:T(8,128)(2,1)S(1)}, bf16[128,1280]{0,1:T(8,128)(2,1)}, u32[]{:S(2)}) copy-start(bf16[128,1280]{0,1:T(8,128)(2,1)} %copy.165) | copy-start | bytes 983044
  124.2 6.2 %collective-permute-start.2 = (bf16[128,512]{0,1:T(8,128)(2,1)}, bf16[128,512]{0,1:T(8,128)(2,1)S(1)}, u32[]{:S(2)}, u32[]{:S(2)}) collective-permute-start(bf16[128,512]{0,1:T(8,128)(2,1)} %collective-permute-done), channel_id=1, source_target_pairs={{0,1},{1,2},{2,3},{3,4},{4,5},{5,6},{6,7},{7,8},{8,9},{9,10},{10,1... | collective-permute-start | bytes 393224 | tf_op jit(solution)/shard_map/ppermute | solution.py:31
  125.7 6.1 %collective-permute-start.3 = (bf16[128,512]{0,1:T(8,128)(2,1)}, bf16[128,512]{0,1:T(8,128)(2,1)S(1)}, u32[]{:S(2)}, u32[]{:S(2)}) collective-permute-start(bf16[128,512]{0,1:T(8,128)(2,1)} %collective-permute-done.1), channel_id=1, source_target_pairs={{0,15},{1,0},{2,1},{3,2},{4,3},{5,4},{6,5},{7,6},{8,7},{9,8},{10,9... | collective-permute-start | bytes 393224 | tf_op jit(solution)/shard_map/ppermute | solution.py:36
  130.3 6.2 %collective-permute-start.4 = (bf16[128,512]{0,1:T(8,128)(2,1)S(1)}, bf16[128,512]{0,1:T(8,128)(2,1)S(1)}, u32[]{:S(2)}, u32[]{:S(2)}) collective-permute-start(bf16[128,512]{0,1:T(8,128)(2,1)S(1)} %collective-permute-done.2), channel_id=1, source_target_pairs={{0,1},{1,2},{2,3},{3,4},{4,5},{5,6},{6,7},{7,8},{8,9},{9,10},{10,1... | collective-permute-start | bytes 393224 | tf_op jit(solution)/shard_map/ppermute | solution.py:31
  131.8 5.2 collective-permute-start.5
  136.6 6.8 %collective-permute-start.6 = (bf16[128,512]{0,1:T(8,128)(2,1)S(1)}, bf16[128,512]{0,1:T(8,128)(2,1)S(1)}, u32[]{:S(2)}, u32[]{:S(2)}) collective-permute-start(bf16[128,512]{0,1:T(8,128)(2,1)S(1)} %collective-permute-done.4), channel_id=1, source_target_pairs={{0,1},{1,2},{2,3},{3,4},{4,5},{5,6},{6,7},{7,8},{8,9},{9,10},{10,1... | collective-permute-start | bytes 393224 | tf_op jit(solution)/shard_map/ppermute | solution.py:31
  137.0 6.3 %collective-permute-start.7 = (bf16[128,512]{0,1:T(8,128)(2,1)S(1)}, bf16[128,512]{0,1:T(8,128)(2,1)S(1)}, u32[]{:S(2)}, u32[]{:S(2)}) collective-permute-start(bf16[128,512]{0,1:T(8,128)(2,1)S(1)} %collective-permute-done.5), channel_id=1, source_target_pairs={{0,15},{1,0},{2,1},{3,2},{4,3},{5,4},{6,5},{7,6},{8,7},{9,8},{10,9... | collective-permute-start | bytes 393224 | tf_op jit(solution)/shard_map/ppermute | solution.py:36
  143.3 7.1 %collective-permute-start.8 = (bf16[128,512]{0,1:T(8,128)(2,1)S(1)}, bf16[128,512]{0,1:T(8,128)(2,1)S(1)}, u32[]{:S(2)}, u32[]{:S(2)}) collective-permute-start(bf16[128,512]{0,1:T(8,128)(2,1)S(1)} %collective-permute-done.6), channel_id=1, source_target_pairs={{0,1},{1,2},{2,3},{3,4},{4,5},{5,6},{6,7},{7,8},{8,9},{9,10},{10,1... | collective-permute-start | bytes 393224 | tf_op jit(solution)/shard_map/ppermute | solution.py:31
  143.4 7.1 %collective-permute-start.9 = (bf16[128,512]{0,1:T(8,128)(2,1)S(1)}, bf16[128,512]{0,1:T(8,128)(2,1)S(1)}, u32[]{:S(2)}, u32[]{:S(2)}) collective-permute-start(bf16[128,512]{0,1:T(8,128)(2,1)S(1)} %collective-permute-done.7), channel_id=1, source_target_pairs={{0,15},{1,0},{2,1},{3,2},{4,3},{5,4},{6,5},{7,6},{8,7},{9,8},{10,9... | collective-permute-start | bytes 393224 | tf_op jit(solution)/shard_map/ppermute | solution.py:36
  150.4 7.1 %collective-permute-start.10 = (bf16[128,512]{0,1:T(8,128)(2,1)S(1)}, bf16[128,512]{0,1:T(8,128)(2,1)S(1)}, u32[]{:S(2)}, u32[]{:S(2)}) collective-permute-start(bf16[128,512]{0,1:T(8,128)(2,1)S(1)} %collective-permute-done.8), channel_id=1, source_target_pairs={{0,1},{1,2},{2,3},{3,4},{4,5},{5,6},{6,7},{7,8},{8,9},{9,10},{10,1... | collective-permute-start | bytes 393224 | tf_op jit(solution)/shard_map/ppermute | solution.py:31
  150.4 7.1 %collective-permute-start.11 = (bf16[128,512]{0,1:T(8,128)(2,1)S(1)}, bf16[128,512]{0,1:T(8,128)(2,1)S(1)}, u32[]{:S(2)}, u32[]{:S(2)}) collective-permute-start(bf16[128,512]{0,1:T(8,128)(2,1)S(1)} %collective-permute-done.9), channel_id=1, source_target_pairs={{0,15},{1,0},{2,1},{3,2},{4,3},{5,4},{6,5},{7,6},{8,7},{9,8},{10,9... | collective-permute-start | bytes 393224 | tf_op jit(solution)/shard_map/ppermute | solution.py:36
  157.5 7.7 %collective-permute-start.12 = (bf16[128,512]{0,1:T(8,128)(2,1)S(1)}, bf16[128,512]{0,1:T(8,128)(2,1)S(1)}, u32[]{:S(2)}, u32[]{:S(2)}) collective-permute-start(bf16[128,512]{0,1:T(8,128)(2,1)S(1)} %collective-permute-done.10), channel_id=1, source_target_pairs={{0,1},{1,2},{2,3},{3,4},{4,5},{5,6},{6,7},{7,8},{8,9},{9,10},{10,1... | collective-permute-start | bytes 393224 | tf_op jit(solution)/shard_map/ppermute | solution.py:31
  157.5 7.7 %collective-permute-start.13 = (bf16[128,512]{0,1:T(8,128)(2,1)S(1)}, bf16[128,512]{0,1:T(8,128)(2,1)S(1)}, u32[]{:S(2)}, u32[]{:S(2)}) collective-permute-start(bf16[128,512]{0,1:T(8,128)(2,1)S(1)} %collective-permute-done.11), channel_id=1, source_target_pairs={{0,15},{1,0},{2,1},{3,2},{4,3},{5,4},{6,5},{7,6},{8,7},{9,8},{10,9... | collective-permute-start | bytes 393224 | tf_op jit(solution)/shard_map/ppermute | solution.py:36
  165.2 7.4 %collective-permute-start.14 = (bf16[128,512]{0,1:T(8,128)(2,1)S(1)}, bf16[128,512]{0,1:T(8,128)(2,1)S(1)}, u32[]{:S(2)}, u32[]{:S(2)}) collective-permute-start(bf16[128,512]{0,1:T(8,128)(2,1)S(1)} %collective-permute-done.12), channel_id=1, source_target_pairs={{0,1},{1,2},{2,3},{3,4},{4,5},{5,6},{6,7},{7,8},{8,9},{9,10},{10,1... | collective-permute-start | bytes 393224 | tf_op jit(solution)/shard_map/ppermute | solution.py:31
  186.2 14.4 %slice-start = ((s8[6553600]{0:T(1024)(128)(4,1)}), s8[2359296]{0:T(1024)(128)(4,1)S(1)}, s32[]{:S(2)}) async-start(s8[6553600]{0:T(1024)(128)(4,1)} %bitcast.131), calls=%async_computation.6 | async-start | bytes 4718592
  192.7 7.9 %slice-start.1 = ((s8[6553600]{0:T(1024)(128)(4,1)}), s8[4194304]{0:T(1024)(128)(4,1)S(1)}, s32[]{:S(2)}) async-start(s8[6553600]{0:T(1024)(128)(4,1)} %bitcast.131), calls=%async_computation.7 | async-start | bytes 8388608
  192.7 7.9 %copy-start.5 = (bf16[128,2560]{1,0:T(8,128)(2,1)S(1)}, bf16[128,2560]{1,0:T(8,128)(2,1)}, u32[]{:S(2)}) copy-start(bf16[128,2560]{1,0:T(8,128)(2,1)} %param.12) | copy-start | bytes 1966084
  205.2 138.2 %copy-start.10 = (bf16[1,2560,768]{2,1,0:T(8,128)(2,1)S(1)}, bf16[1,2560,768]{2,1,0:T(8,128)(2,1)}, u32[]{:S(2)}) copy-start(bf16[1,2560,768]{2,1,0:T(8,128)(2,1)} %param.21) | copy-start | bytes 11796484
  339.6 3.8 copy-start.2
  382.5 7.2 %copy-start.9 = (s32[128,6]{0,1:T(8,128)S(1)}, s32[128,6]{0,1:T(8,128)}, u32[]{:S(2)}) copy-start(s32[128,6]{0,1:T(8,128)} %param.20) | copy-start | bytes 9220
  382.5 7.4 %copy-start.7 = (pred[128,64]{0,1:T(8,128)(4,1)S(1)}, pred[128,64]{0,1:T(8,128)(4,1)}, u32[]{:S(2)}) copy-start(pred[128,64]{0,1:T(8,128)(4,1)} %get-tuple-element.16) | copy-start | bytes 24580
  382.5 148.9 %all-to-all-start.4 = ((bf16[128,16,2560]{2,1,0:T(8,128)(2,1)}), bf16[128,16,2560]{2,1,0:T(8,128)(2,1)}, u32[]{:S(2)}, u32[]{:S(2)}) async-start(bf16[128,16,2560]{2,1,0:T(8,128)(2,1)} %bitcast.135), calls=%async_computation.4 | async-start | bytes 20971520 | tf_op jit(solution)/shard_map/all_to_all | solution.py:211
Sparse Core Ops, SparseCore 0:
  9.0 31.9 all-gather.1
